TPU v7x, 32 devices: a whole 2x2x4 slice. The times are simulated.
32 devices in a mesh: pair: 4 (over z), gen: 8 (over y, x, core).
Axes of the slice: x: 2, y: 2, z: 4, core: 2. Of those that a mesh axis runs over, the one named last changes fastest.
Arguments:
- tokens: bfloat16 [32768, 2048], P(('pair', 'gen')), may hold values from -6 to 6
- cotangent: bfloat16 [32768, 256], P(('pair', 'gen')), may hold values from -6 to 6
- block_pair: int32 [32, 1], replicated, may hold values from 0 to 15
- src_lang: int32 [16], replicated, may hold values from 0 to 95
- tgt_lang: int32 [16], replicated, may hold values from 0 to 95
- lang_embed: float32 [96, 512], P(None, 'pair'), may hold values from -5 to 5
- generator: bfloat16 [512, 524288], P('pair', 'gen'), may hold values from -0.005859375 to 0.005859375
Outputs:
- grad_tokens: bfloat16 [32768, 2048], P(('pair', 'gen'))
- grad_generator: bfloat16 [512, 524288], P('pair', 'gen')
- grad_embed: float32 [96, 512], P(None, 'pair')
Inputs may be any that keep to these rules, and one draw needn't show every extreme that they name: `block_pair`: every pair owns at least one block; block counts per pair are uneven.
All inputs are finite; a program needn't handle non-finite values.
Results may differ from a plain program's by a relative error of at most 0.007.
Values may be sent and summed in bfloat16 or wider, within the bound.
No kernel may reach another device: no remote copies, remote signals or barrier semaphores. Data moves between devices by JAX's collectives and lax.ppermute only.
A program may use at most 128 MiB of HBM per device.

v0:
```python
import jax
import jax.numpy as jnp
from jax import lax
from jax.sharding import PartitionSpec as P

BLK = 1024


def shards(tokens, cotangent, block_pair, src_lang, tgt_lang, lang_embed, generator):
    gen_count = lax.axis_size("gen")
    pair_index = lax.axis_index("pair")
    blocks_here = tokens.shape[0] // BLK
    model_width = tokens.shape[1]
    adapter_rank = cotangent.shape[1]
    languages = lang_embed.shape[0]
    pair_count = src_lang.shape[0]
    lang_ids = jnp.arange(languages, dtype=jnp.int32)
    hot_both = (src_lang[:, None] == lang_ids[None, :]).astype(jnp.float32) + (
        tgt_lang[:, None] == lang_ids[None, :]
    ).astype(jnp.float32)
    pair_embed = jnp.dot(hot_both, lang_embed, precision=lax.Precision.HIGHEST).astype(jnp.bfloat16)
    partial_value = jnp.dot(pair_embed, generator, preferred_element_type=jnp.float32)
    adapter_cols = lax.psum(partial_value, "pair").astype(jnp.bfloat16)
    flat_pairs = block_pair[:, 0]
    row_pairs = lax.dynamic_slice_in_dim(
        flat_pairs, pair_index * (gen_count * blocks_here), gen_count * blocks_here
    )
    send_order = row_pairs.reshape(gen_count, blocks_here).T
    outgoing = jnp.take(adapter_cols, send_order, axis=0).reshape(
        blocks_here, gen_count * adapter_cols.shape[1]
    )
    own_adapters = lax.all_to_all(outgoing, "gen", split_axis=1, concat_axis=1, tiled=True)
    adapters = own_adapters.reshape(blocks_here, model_width, adapter_rank)
    token_blocks = tokens.reshape(blocks_here, BLK, model_width)
    cot_blocks = cotangent.reshape(blocks_here, BLK, adapter_rank)
    hidden = jnp.einsum("btd,bdr->btr", token_blocks, adapters, preferred_element_type=jnp.float32)
    logistic = jax.nn.sigmoid(hidden)
    grad_hidden = (
        cot_blocks.astype(jnp.float32) * logistic * (1.0 + hidden * (1.0 - logistic))
    ).astype(jnp.bfloat16)
    grad_tokens = (
        jnp.einsum("btr,bdr->btd", grad_hidden, adapters, preferred_element_type=jnp.float32)
        .astype(jnp.bfloat16)
        .reshape(tokens.shape)
    )
    outer_grads = jnp.einsum(
        "btd,btr->bdr", token_blocks, grad_hidden, preferred_element_type=jnp.float32
    ).reshape(blocks_here, model_width * adapter_rank)
    returned = lax.all_to_all(outer_grads, "gen", split_axis=1, concat_axis=0, tiled=True)
    pair_ids = jnp.arange(pair_count, dtype=jnp.int32)
    segment_hot = (pair_ids[:, None] == row_pairs[None, :]).astype(jnp.float32)
    row_grad = jnp.dot(segment_hot, returned, precision=lax.Precision.HIGHEST)
    grad_rounded = lax.psum(row_grad, "pair").astype(jnp.bfloat16)
    grad_generator = jnp.einsum(
        "pe,pc->ec", pair_embed, grad_rounded, preferred_element_type=jnp.float32
    ).astype(jnp.bfloat16)
    partial_pair = jnp.einsum(
        "pc,ec->pe", grad_rounded, generator, preferred_element_type=jnp.float32
    )
    grad_pair = lax.psum(partial_pair, "gen")
    grad_embed = jnp.dot(hot_both.T, grad_pair, precision=lax.Precision.HIGHEST)
    return (grad_tokens, grad_generator, grad_embed)


def solution(mesh):
    placed = (
        P(("pair", "gen"), None),
        P(("pair", "gen"), None),
        P(),
        P(),
        P(),
        P(None, "pair"),
        P("pair", "gen"),
    )
    return jax.shard_map(
        shards,
        mesh=mesh,
        in_specs=placed,
        out_specs=(P(("pair", "gen"), None), P("pair", "gen"), P(None, "pair")),
        check_vma=False,
    )
```

profile of v0, /device:TPU:0, one launch (start us, length us, event | category | flops | bytes accessed | tf_op | source)
XLA Modules:
  0.0 421.6 jit_solution(15591775119214140472)
XLA Ops:
  0.6 0.0 copy-start
  0.7 0.7 fusion.16
  1.4 0.7 compare_and_fusion
  2.1 0.0 copy-done
  2.1 0.9 convolution_convert_fusion.2
  3.0 10.1 %fusion.21 = f32[16,65536]{1,0:T(8,128)} fusion(bf16[16,128]{1,0:T(8,128)(2,1)S(1)} %convolution_convert_fusion.2, bf16[128,65536]{1,0:T(8,128)(2,1)} %param.13), kind=kOutput, calls=%fused_computation.39 | convolution fusion | flops 268435456 | bytes 20975616 | tf_op jit(solution)/shard_map/dot_general | solution.py:22
  13.1 149.0 %all-reduce.2 = bf16[16,65536]{1,0:T(8,128)(2,1)S(1)} all-reduce(f32[16,65536]{1,0:T(8,128)} %fusion.21), channel_id=1, replica_groups=mesh['pair'=4,'gen'=8] {'pair'}, use_global_device_ids=true, to_apply=%region_0.0 | all-reduce | flops 1048576 | bytes 6291456 | tf_op jit(solution)/shard_map/psum | solution.py:23
  162.1 1.2 gather_fusion
  163.4 0.2 bitcast_select_fusion
  163.5 1.6 copy.27
  165.2 0.5 broadcast.100
  165.7 7.0 %reduce.2 = bf16[8,65536]{1,0:T(8,128)(2,1)S(1)} reduce(bf16[8,1,65536]{2,1,0:T(2,128)(2,1)S(1)} %bitcast.33, bf16[]{:T(256)} %broadcast.100), dimensions={1}, to_apply=%bitcast.32.reduce_sub_computation | reduce | bytes 2097154
  172.7 0.0 copy-start.4
  172.7 1.9 reshape.166
  174.6 3.8 all-to-all-start
  178.4 0.0 copy-done.4
  178.4 1.0 copy.17
  179.4 14.3 %all-to-all-done = bf16[8,2,32768]{2,1,0:T(2,128)(2,1)S(1)} async-done(((bf16[8,2,32768]{2,1,0:T(2,128)(2,1)}), bf16[8,2,32768]{2,1,0:T(2,128)(2,1)S(1)}, u32[]{:S(2)}, u32[]{:S(2)}) %all-to-all-start) | async-done | bytes 1048608 | tf_op jit(solution)/shard_map/all_to_all | solution.py:32
  193.7 1.0 reshape.167
  194.8 6.0 %bitcast_reduce_fusion = bf16[8,65536]{1,0:T(8,128)(2,1)S(1)} fusion(bf16[8,1,65536]{2,1,0:T(2,128)(2,1)S(1)} %reshape.167), kind=kLoop, calls=%fused_computation.37 | loop fusion | bytes 2097152 | tf_op jit(solution)/shard_map/all_to_all | solution.py:32
  200.8 0.5 reshape.156
  201.3 0.0 copy-start.2
  201.3 0.0 copy-start.5
  201.3 0.0 copy-start.6
  201.3 3.9 convolution_bitcast_fusion.1
  205.2 0.0 copy-done.2
  205.2 0.0 copy-start.9
  205.2 1.0 copy-done.9
  206.2 0.0 copy-done.5
  206.2 0.0 copy-done.6
  206.2 2.9 convolution_bitcast_fusion
  209.1 1.9 copy.19
  211.0 0.0 copy-start.3
  211.0 4.2 all_to_all.20
  215.2 3.9 all-to-all-start.1
  219.0 0.0 copy-done.3
  219.0 5.0 %convolution_convert_fusion.1 = bf16[1024,2048]{1,0:T(8,128)(2,1)} fusion(bf16[2048,256]{1,0:T(8,128)(2,1)S(1)} %copy-done.3, f32[1024,256]{0,1:T(8,128)} %copy-done.9, bf16[1024,256]{0,1:T(8,128)(2,1)} %copy.17), kind=kOutput, calls=%fused_computation.2 | convolution fusion | flops 1078460416 | bytes 6815744 | tf_op jit(solution)/shard_map/btr,bdr->btd/dot_general | solution.py:42
  224.0 21.3 %all-to-all-done.1 = f32[1,8,65536]{2,0,1:T(1,128)S(1)} async-done(((f32[1,8,65536]{2,0,1:T(1,128)}), f32[1,8,65536]{2,0,1:T(1,128)S(1)}, u32[]{:S(2)}, u32[]{:S(2)}) %all-to-all-start.1) | async-done | bytes 2097184 | tf_op jit(solution)/shard_map/all_to_all | solution.py:49
  245.3 4.8 %fusion = f32[16,65536]{1,0:T(8,128)} fusion(f32[1,8,65536]{2,0,1:T(1,128)S(1)} %all-to-all-done.1, s32[8]{0:T(128)S(1)} %get-tuple-element.4), kind=kOutput, calls=%fused_computation.4 | convolution fusion | flops 100663424 | bytes 6291488 | tf_op jit(solution)/shard_map/dot_general | solution.py:52
  250.1 141.2 %all-reduce.3 = bf16[16,65536]{1,0:T(8,128)(2,1)S(1)} all-reduce(f32[16,65536]{1,0:T(8,128)} %fusion), channel_id=1, replica_groups=mesh['pair'=4,'gen'=8] {'pair'}, use_global_device_ids=true, to_apply=%region_1.2 | all-reduce | flops 1048576 | bytes 6291456 | tf_op jit(solution)/shard_map/psum | solution.py:53
  391.4 8.5 %convolution_convert_fusion = bf16[128,65536]{1,0:T(8,128)(2,1)} fusion(bf16[16,128]{1,0:T(8,128)(2,1)S(1)} %convolution_convert_fusion.2, bf16[16,65536]{1,0:T(8,128)(2,1)S(1)} %all-reduce.3), kind=kOutput, calls=%fused_computation.1 | convolution fusion | flops 276824064 | bytes 18878464 | tf_op jit(solution)/shard_map/pe,pc->ec/dot_general | solution.py:54
  399.9 0.0 copy-start.7
  399.9 8.1 %fusion.22 = f32[16,128]{1,0:T(8,128)S(1)} fusion(bf16[16,65536]{1,0:T(8,128)(2,1)S(1)} %all-reduce.3, bf16[128,65536]{1,0:T(8,128)(2,1)} %param.13), kind=kOutput, calls=%fused_computation.40 | convolution fusion | flops 268435456 | bytes 18882560 | tf_op jit(solution)/shard_map/pc,ec->pe/dot_general | solution.py:57
  408.0 12.6 %psum.23 = f32[16,128]{1,0:T(8,128)S(1)} all-reduce(f32[16,128]{1,0:T(8,128)S(1)} %fusion.22), channel_id=1, replica_groups=mesh['pair'=4,'gen'=8] {'gen'}, use_global_device_ids=true, to_apply=%region_2.3 | all-reduce | flops 2048 | bytes 16384 | tf_op jit(solution)/shard_map/psum | solution.py:60
  420.6 0.0 copy-done.7
  420.6 0.0 copy-done.8
  420.6 1.0 fusion.10
  421.6 0.0 copy-done.1
  (3 shorter events, 0.0 us)
Async XLA Ops:
  0.6 1.5 copy-start
  172.7 5.7 %copy-start.4 = (bf16[1024,256]{1,0:T(8,128)(2,1)S(1)}, bf16[1024,256]{1,0:T(8,128)(2,1)}, u32[]{:S(2)}) copy-start(bf16[1024,256]{1,0:T(8,128)(2,1)} %param.8) | copy-start | bytes 1572868
  174.6 19.1 %all-to-all-start = ((bf16[8,2,32768]{2,1,0:T(2,128)(2,1)}), bf16[8,2,32768]{2,1,0:T(2,128)(2,1)S(1)}, u32[]{:S(2)}, u32[]{:S(2)}) async-start(bf16[8,2,32768]{2,1,0:T(2,128)(2,1)} %reshape.166), calls=%async_computation | async-start | bytes 2097152 | tf_op jit(solution)/shard_map/all_to_all | solution.py:32
  201.3 3.9 copy-start.2
  201.3 4.9 %copy-start.5 = (bf16[1024,256]{0,1:T(8,128)(2,1)S(1)}, bf16[1024,256]{0,1:T(8,128)(2,1)}, u32[]{:S(2)}) copy-start(bf16[1024,256]{0,1:T(8,128)(2,1)} %copy.17) | copy-start | bytes 1572868
  201.3 4.9 %copy-start.6 = (bf16[1024,2048]{1,0:T(8,128)(2,1)S(1)}, bf16[1024,2048]{1,0:T(8,128)(2,1)}, u32[]{:S(2)}) copy-start(bf16[1024,2048]{1,0:T(8,128)(2,1)} %param.7) | copy-start | bytes 12582916
  205.2 1.0 copy-start.9
  211.0 8.0 %copy-start.3 = (bf16[2048,256]{1,0:T(8,128)(2,1)S(1)}, bf16[2048,256]{1,0:T(8,128)(2,1)}, u32[]{:S(2)}) copy-start(bf16[2048,256]{1,0:T(8,128)(2,1)} %copy-done.2) | copy-start | bytes 3145732
  215.2 30.2 %all-to-all-start.1 = ((f32[1,8,65536]{2,0,1:T(1,128)}), f32[1,8,65536]{2,0,1:T(1,128)S(1)}, u32[]{:S(2)}, u32[]{:S(2)}) async-start(f32[1,8,65536]{2,0,1:T(1,128)} %all_to_all.20), calls=%async_computation.1 | async-start | bytes 4194304 | tf_op jit(solution)/shard_map/all_to_all | solution.py:49
  399.9 20.7 %copy-start.7 = (s32[16]{0:T(128)S(1)}, s32[16]{0:T(128)}, u32[]{:S(2)}) copy-start(s32[16]{0:T(128)} %param.11) | copy-start | bytes 196
  399.9 20.7 %copy-start.8 = (s32[16]{0:T(128)S(1)}, s32[16]{0:T(128)}, u32[]{:S(2)}) copy-start(s32[16]{0:T(128)} %param.10) | copy-start | bytes 196
  399.9 21.7 %copy-start.1 = (f32[96,128]{1,0:T(8,128)S(1)}, f32[96,128]{1,0:T(8,128)}, u32[]{:S(2)}) copy-start(f32[96,128]{1,0:T(8,128)} %param.12) | copy-start | bytes 147460
where the time goes:
time: 422 us
  blocking collectives  303 us (72%)
  matrix products  45.1 us (11%)
  waiting for transfers between devices  35.7 us (8%)
  local copies, waits for them, and re-layouts  20.8 us (5%)
  other arithmetic  8.67 us (2%)
  starting transfers between devices  7.64 us (2%)
    psum x1, blocking collectives, shards(): adapter_cols = lax.psum(partial_value, 'pair').astype(jnp.bfloat16)  149 us
    psum x1, blocking collectives, shards(): grad_rounded = lax.psum(row_grad, 'pair').astype(jnp.bfloat16)  141 us
    all_to_all x1, waiting for transfers between devices, shards(): lax.all_to_all(outer_grads, 'gen', split_axis=1, concat_axis=0, tiled=True)  21.3 us
    all_to_all x1, waiting for transfers between devices, shards(): lax.all_to_all(outgoing, 'gen', split_axis=1, concat_axis=1, tiled=True)  14.3 us
    psum x1, blocking collectives, shards(): grad_pair = lax.psum(partial_pair, 'gen')  12.6 us
    dot_general x1, matrix products, shards(): jnp.dot(pair_embed, generator, preferred_element_type=jnp.float32)  10.1 us
    dot_general x1, matrix products, shards(): jnp.einsum('pe,pc->ec', pair_embed, grad_rounded, preferred_element_type=...  8.55 us
  transfers between devices with their start and end apart: 2, of which 2 were waited for; matrix products, arithmetic and copies ran while one was open for 1% of the time, Pallas kernels for 0%

commit v1 on v0

--- a/solution.py
+++ b/solution.py
@@ -4,6 +4,22 @@
 from jax.sharding import PartitionSpec as P
 
 BLK = 1024
+
+
+def exchange_in_pairs(shard, axis, split, join):
+    ways, here = (lax.axis_size(axis), lax.axis_index(axis))
+    width = shard.shape[split] // ways
+    dims = list(shard.shape)
+    dims[split] = width
+    height = dims[join]
+    dims[join] = height * ways
+    full = jnp.zeros(dims, shard.dtype)
+    for mask in range(ways):
+        part = lax.dynamic_slice_in_dim(shard, (here ^ mask) * width, width, axis=split)
+        if mask:
+            part = lax.ppermute(part, axis, [(d, d ^ mask) for d in range(ways)])
+        full = lax.dynamic_update_slice_in_dim(full, part, (here ^ mask) * height, axis=join)
+    return full
 
 
 def shards(tokens, cotangent, block_pair, src_lang, tgt_lang, lang_embed, generator):
@@ -29,7 +45,7 @@
     outgoing = jnp.take(adapter_cols, send_order, axis=0).reshape(
         blocks_here, gen_count * adapter_cols.shape[1]
     )
-    own_adapters = lax.all_to_all(outgoing, "gen", split_axis=1, concat_axis=1, tiled=True)
+    own_adapters = exchange_in_pairs(outgoing, "gen", 1, 1)
     adapters = own_adapters.reshape(blocks_here, model_width, adapter_rank)
     token_blocks = tokens.reshape(blocks_here, BLK, model_width)
     cot_blocks = cotangent.reshape(blocks_here, BLK, adapter_rank)

time: 422 us -> 450 us (1.066)
  other arithmetic: 8.67 us -> 28.4 us
  local copies, waits for them, and re-layouts: 20.8 us -> 25.7 us
    dynamic_update_slice x0 -> x1, other arithmetic: none -> 22 us  [exchange_in_pairs(): lax.dynamic_update_slice_in_dim(full, part, (here ^ mask) * height, axis=...]
    all_to_all x1 -> x0, waiting for transfers between devices: 14.3 us -> none  [shards(): lax.all_to_all(outgoing, 'gen', split_axis=1, concat_axis=1, tiled=True)]
    ppermute x0 -> x7, waiting for transfers between devices: none -> 13.1 us  [exchange_in_pairs(): part = lax.ppermute(part, axis, [(d, d ^ mask) for d in range(ways)])]
    ppermute x0 -> x7, starting transfers between devices: none -> 7.33 us  [exchange_in_pairs(): part = lax.ppermute(part, axis, [(d, d ^ mask) for d in range(ways)])]
    unnamed x1 -> x0, other arithmetic: 7.03 us -> none
    dynamic_update_slice x0 -> x7, local copies, waits for them, and re-layouts: none -> 6.75 us  [exchange_in_pairs(): lax.dynamic_update_slice_in_dim(full, part, (here ^ mask) * height, axis=...]
    all_to_all x1 -> x0, local copies, waits for them, and re-layouts: 5.99 us -> none  [shards(): lax.all_to_all(outgoing, 'gen', split_axis=1, concat_axis=1, tiled=True)]
    select_n x2, other arithmetic: 0.9 us -> 5.72 us  [shards(): jnp.take(adapter_cols, send_order, axis=0)]
  transfers between devices with their start and end apart: 2 -> 8, of which waited for: 2 -> 4; matrix products, arithmetic and copies ran while one was open for 1% -> 3% of each run, Pallas kernels for 0% -> 0%
where the time goes in v1:
time: 450 us
  blocking collectives  303 us (67%)
  matrix products  45.1 us (10%)
  waiting for transfers between devices  34.8 us (8%)
  other arithmetic  28.4 us (6%)
  local copies, waits for them, and re-layouts  25.7 us (6%)
  starting transfers between devices  11.7 us (3%)
    psum x1, blocking collectives, shards(): adapter_cols = lax.psum(partial_value, 'pair').astype(jnp.bfloat16)  149 us
    psum x1, blocking collectives, shards(): grad_rounded = lax.psum(row_grad, 'pair').astype(jnp.bfloat16)  141 us
    dynamic_update_slice x1, other arithmetic, exchange_in_pairs(): lax.dynamic_update_slice_in_dim(full, part, (here ^ mask) * height, axis=...  22 us
    all_to_all x1, waiting for transfers between devices, shards(): lax.all_to_all(outer_grads, 'gen', split_axis=1, concat_axis=0, tiled=True)  21.7 us
    ppermute x7, waiting for transfers between devices, exchange_in_pairs(): part = lax.ppermute(part, axis, [(d, d ^ mask) for d in range(ways)])  13.1 us
    psum x1, blocking collectives, shards(): grad_pair = lax.psum(partial_pair, 'gen')  12.4 us
    dot_general x1, matrix products, shards(): jnp.dot(pair_embed, generator, preferred_element_type=jnp.float32)  10.1 us
  transfers between devices with their start and end apart: 8, of which 4 were waited for; matrix products, arithmetic and copies ran while one was open for 3% of the time, Pallas kernels for 0%

profile of v1, /device:TPU:0, one launch (start us, length us, event | category | flops | bytes accessed | tf_op | source)
XLA Modules:
  0.0 449.5 jit_solution(9677962106880586276)
XLA Ops:
  0.6 0.0 copy-start
  0.7 0.7 fusion.16
  1.4 0.7 compare_and_fusion
  2.2 0.9 convolution_convert_fusion.2
  3.0 10.1 %fusion.21 = f32[16,65536]{1,0:T(8,128)} fusion(bf16[16,128]{1,0:T(8,128)(2,1)S(1)} %convolution_convert_fusion.2, bf16[128,65536]{1,0:T(8,128)(2,1)} %param.13), kind=kOutput, calls=%fused_computation.53 | convolution fusion | flops 268435456 | bytes 20975616 | tf_op jit(solution)/shard_map/dot_general | solution.py:38
  13.1 149.0 %all-reduce.2 = bf16[16,65536]{1,0:T(8,128)(2,1)S(1)} all-reduce(f32[16,65536]{1,0:T(8,128)} %fusion.21), channel_id=1, replica_groups=mesh['pair'=4,'gen'=8] {'pair'}, use_global_device_ids=true, to_apply=%region_0.0 | all-reduce | flops 1048576 | bytes 6291456 | tf_op jit(solution)/shard_map/psum | solution.py:39
  162.1 1.2 gather_fusion
  163.4 2.9 copy.18
  166.3 0.2 broadcast_bitcast_fusion
  166.5 1.9 copy.17
  168.5 5.0 %broadcast_select_fusion = bf16[1,524288]{1,0:T(2,128)(2,1)S(1)} fusion(pred[1,524288]{1,0:T(4,128)(4,1)S(1)} %bitcast.33, bf16[1,524288]{1,0:T(2,128)(2,1)} %bitcast.34), kind=kLoop, calls=%fused_computation.15 | loop fusion | flops 524288 | bytes 2621440 | tf_op jit(solution)/shard_map/jit(_take)/select_n | solution.py:45
  173.5 1.1 broadcast_in_dim.21
  174.6 0.0 copy-start.4
  174.6 3.1 constant_dynamic-slice_fusion
  177.7 1.5 collective-permute-start.1
  179.2 0.4 collective-permute-start.2
  179.5 1.5 collective-permute-start.3
  181.1 0.1 collective-permute-start.4
  181.2 1.0 copy.13
  182.2 2.4 collective-permute-start.5
  184.7 1.2 constant_dynamic-update-slice_fusion.5
  185.9 1.2 collective-permute-done.1
  187.1 1.4 collective-permute-start.6
  188.5 1.2 constant_dynamic-update-slice_fusion.4
  189.7 2.2 collective-permute-done.2
  192.0 1.2 constant_dynamic-update-slice_fusion.3
  193.2 1.2 constant_dynamic-update-slice_fusion.2
  194.4 9.7 %collective-permute-done.4 = bf16[1,65536]{1,0:T(2,128)(2,1)} collective-permute-done((bf16[1,65536]{1,0:T(2,128)(2,1)S(1)}, bf16[1,65536]{1,0:T(2,128)(2,1)}, u32[]{:S(2)}, u32[]{:S(2)}) %collective-permute-start.4) | collective-permute-done | bytes 131104 | tf_op jit(solution)/shard_map/ppermute | solution.py:20
  204.1 1.2 constant_dynamic-update-slice_fusion.1
  205.4 0.3 constant_dynamic-update-slice_fusion
  205.7 0.3 constant_dynamic-update-slice_fusion.6
  206.0 22.0 %reduce = bf16[524288]{0:T(1024)(128)(2,1)S(1)} reduce(bf16[1,524288]{1,0:T(2,128)(2,1)S(1)} %constant_dynamic-update-slice_fusion.6, bf16[]{:T(256)} %constant.52), dimensions={0}, to_apply=%dynamic_update_slice.31.reduce_sub_computation | reduce | bytes 2097154 | tf_op jit(solution)/shard_map/dynamic_update_slice | solution.py:21
  228.0 0.4 reshape.149
  228.4 0.0 copy-start.6
  228.4 3.9 convolution_bitcast_fusion.1
  232.3 1.0 copy-done.9
  233.3 2.9 convolution_bitcast_fusion
  236.2 1.9 copy.14
  238.1 4.2 all_to_all.15
  242.2 4.3 all-to-all-start
  246.6 5.0 %convolution_convert_fusion.1 = bf16[1024,2048]{1,0:T(8,128)(2,1)} fusion(bf16[2048,256]{1,0:T(8,128)(2,1)S(1)} %copy-done.3, f32[1024,256]{0,1:T(8,128)} %copy-done.9, bf16[1024,256]{0,1:T(8,128)(2,1)} %copy.13), kind=kOutput, calls=%fused_computation.2 | convolution fusion | flops 1078460416 | bytes 6815744 | tf_op jit(solution)/shard_map/btr,bdr->btd/dot_general | solution.py:58
  251.6 21.7 %all-to-all-done = f32[1,8,65536]{2,0,1:T(1,128)S(1)} async-done(((f32[1,8,65536]{2,0,1:T(1,128)}), f32[1,8,65536]{2,0,1:T(1,128)S(1)}, u32[]{:S(2)}, u32[]{:S(2)}) %all-to-all-start) | async-done | bytes 2097184 | tf_op jit(solution)/shard_map/all_to_all | solution.py:65
  273.2 4.8 %fusion = f32[16,65536]{1,0:T(8,128)} fusion(f32[1,8,65536]{2,0,1:T(1,128)S(1)} %all-to-all-done, s32[8]{0:T(128)S(1)} %get-tuple-element.4), kind=kOutput, calls=%fused_computation.4 | convolution fusion | flops 100663424 | bytes 6291488 | tf_op jit(solution)/shard_map/dot_general | solution.py:68
  278.0 141.5 %all-reduce.3 = bf16[16,65536]{1,0:T(8,128)(2,1)S(1)} all-reduce(f32[16,65536]{1,0:T(8,128)} %fusion), channel_id=1, replica_groups=mesh['pair'=4,'gen'=8] {'pair'}, use_global_device_ids=true, to_apply=%region_1.2 | all-reduce | flops 1048576 | bytes 6291456 | tf_op jit(solution)/shard_map/psum | solution.py:69
  419.5 8.5 %convolution_convert_fusion = bf16[128,65536]{1,0:T(8,128)(2,1)} fusion(bf16[16,128]{1,0:T(8,128)(2,1)S(1)} %convolution_convert_fusion.2, bf16[16,65536]{1,0:T(8,128)(2,1)S(1)} %all-reduce.3), kind=kOutput, calls=%fused_computation.1 | convolution fusion | flops 276824064 | bytes 18878464 | tf_op jit(solution)/shard_map/pe,pc->ec/dot_general | solution.py:70
  428.0 8.1 %fusion.22 = f32[16,128]{1,0:T(8,128)S(1)} fusion(bf16[16,65536]{1,0:T(8,128)(2,1)S(1)} %all-reduce.3, bf16[128,65536]{1,0:T(8,128)(2,1)} %param.13), kind=kOutput, calls=%fused_computation.54 | convolution fusion | flops 268435456 | bytes 18882560 | tf_op jit(solution)/shard_map/pc,ec->pe/dot_general | solution.py:73
  436.1 12.4 %psum.23 = f32[16,128]{1,0:T(8,128)S(1)} all-reduce(f32[16,128]{1,0:T(8,128)S(1)} %fusion.22), channel_id=1, replica_groups=mesh['pair'=4,'gen'=8] {'gen'}, use_global_device_ids=true, to_apply=%region_2.3 | all-reduce | flops 2048 | bytes 16384 | tf_op jit(solution)/shard_map/psum | solution.py:76
  448.5 1.0 fusion.10
  (22 shorter events, 0.0 us)
Async XLA Ops:
  0.6 1.5 copy-start
  174.6 6.6 %copy-start.4 = (bf16[1024,256]{1,0:T(8,128)(2,1)S(1)}, bf16[1024,256]{1,0:T(8,128)(2,1)}, u32[]{:S(2)}) copy-start(bf16[1024,256]{1,0:T(8,128)(2,1)} %param.8) | copy-start | bytes 1572868
  177.7 4.5 %collective-permute-start = (bf16[1,65536]{1,0:T(2,128)(2,1)}, bf16[1,65536]{1,0:T(2,128)(2,1)}, u32[]{:S(2)}, u32[]{:S(2)}) collective-permute-start(bf16[1,65536]{1,0:T(2,128)(2,1)} %get-tuple-element.11), channel_id=1, source_target_pairs={{0,1},{1,0},{2,3},{3,2},{4,5},{5,4},{6,7},{7,6},{8,9},{9,8},{10,11... | collective-permute-start | bytes 393224 | tf_op jit(solution)/shard_map/ppermute | solution.py:20
  177.7 9.4 %collective-permute-start.1 = (bf16[1,65536]{1,0:T(2,128)(2,1)}, bf16[1,65536]{1,0:T(2,128)(2,1)}, u32[]{:S(2)}, u32[]{:S(2)}) collective-permute-start(bf16[1,65536]{1,0:T(2,128)(2,1)} %get-tuple-element.10), channel_id=1, source_target_pairs={{0,2},{1,3},{2,0},{3,1},{4,6},{5,7},{6,4},{7,5},{8,10},{9,11},{10,... | collective-permute-start | bytes 393224 | tf_op jit(solution)/shard_map/ppermute | solution.py:20
  179.2 12.8 %collective-permute-start.2 = (bf16[1,65536]{1,0:T(2,128)(2,1)}, bf16[1,65536]{1,0:T(2,128)(2,1)}, u32[]{:S(2)}, u32[]{:S(2)}) collective-permute-start(bf16[1,65536]{1,0:T(2,128)(2,1)} %get-tuple-element.9), channel_id=1, source_target_pairs={{0,3},{1,2},{2,1},{3,0},{4,7},{5,6},{6,5},{7,4},{8,11},{9,10},{10,... | collective-permute-start | bytes 393224 | tf_op jit(solution)/shard_map/ppermute | solution.py:20
  179.5 13.6 %collective-permute-start.3 = (bf16[1,65536]{1,0:T(2,128)(2,1)}, bf16[1,65536]{1,0:T(2,128)(2,1)}, u32[]{:S(2)}, u32[]{:S(2)}) collective-permute-start(bf16[1,65536]{1,0:T(2,128)(2,1)} %get-tuple-element.8), channel_id=1, source_target_pairs={{0,4},{1,5},{2,6},{3,7},{4,0},{5,1},{6,2},{7,3},{8,12},{9,13},{10,... | collective-permute-start | bytes 393224 | tf_op jit(solution)/shard_map/ppermute | solution.py:20
  181.1 23.1 %collective-permute-start.4 = (bf16[1,65536]{1,0:T(2,128)(2,1)S(1)}, bf16[1,65536]{1,0:T(2,128)(2,1)}, u32[]{:S(2)}, u32[]{:S(2)}) collective-permute-start(bf16[1,65536]{1,0:T(2,128)(2,1)S(1)} %get-tuple-element.7), channel_id=1, source_target_pairs={{0,5},{1,4},{2,7},{3,6},{4,1},{5,0},{6,3},{7,2},{8,13},{9,12},{10,... | collective-permute-start | bytes 393224 | tf_op jit(solution)/shard_map/ppermute | solution.py:20
  182.2 23.2 %collective-permute-start.5 = (bf16[1,65536]{1,0:T(2,128)(2,1)S(1)}, bf16[1,65536]{1,0:T(2,128)(2,1)S(1)}, u32[]{:S(2)}, u32[]{:S(2)}) collective-permute-start(bf16[1,65536]{1,0:T(2,128)(2,1)S(1)} %get-tuple-element.6), channel_id=1, source_target_pairs={{0,6},{1,7},{2,4},{3,5},{4,2},{5,3},{6,0},{7,1},{8,14},{9,15},{10,... | collective-permute-start | bytes 393224 | tf_op jit(solution)/shard_map/ppermute | solution.py:20
  187.1 18.6 %collective-permute-start.6 = (bf16[1,65536]{1,0:T(2,128)(2,1)S(1)}, bf16[1,65536]{1,0:T(2,128)(2,1)S(1)}, u32[]{:S(2)}, u32[]{:S(2)}) collective-permute-start(bf16[1,65536]{1,0:T(2,128)(2,1)S(1)} %get-tuple-element.5), channel_id=1, source_target_pairs={{0,7},{1,6},{2,5},{3,4},{4,3},{5,2},{6,1},{7,0},{8,15},{9,14},{10,... | collective-permute-start | bytes 393224 | tf_op jit(solution)/shard_map/ppermute | solution.py:20
  228.4 3.9 copy-start.2
  228.4 4.9 %copy-start.5 = (bf16[1024,256]{0,1:T(8,128)(2,1)S(1)}, bf16[1024,256]{0,1:T(8,128)(2,1)}, u32[]{:S(2)}) copy-start(bf16[1024,256]{0,1:T(8,128)(2,1)} %copy.13) | copy-start | bytes 1572868
  228.4 4.9 %copy-start.6 = (bf16[1024,2048]{1,0:T(8,128)(2,1)S(1)}, bf16[1024,2048]{1,0:T(8,128)(2,1)}, u32[]{:S(2)}) copy-start(bf16[1024,2048]{1,0:T(8,128)(2,1)} %param.7) | copy-start | bytes 12582916
  232.3 1.0 copy-start.9
  242.2 4.3 copy-start.3
  242.2 31.0 %all-to-all-start = ((f32[1,8,65536]{2,0,1:T(1,128)}), f32[1,8,65536]{2,0,1:T(1,128)S(1)}, u32[]{:S(2)}, u32[]{:S(2)}) async-start(f32[1,8,65536]{2,0,1:T(1,128)} %all_to_all.15), calls=%async_computation | async-start | bytes 4194304 | tf_op jit(solution)/shard_map/all_to_all | solution.py:65
  428.0 20.5 %copy-start.7 = (s32[16]{0:T(128)S(1)}, s32[16]{0:T(128)}, u32[]{:S(2)}) copy-start(s32[16]{0:T(128)} %param.11) | copy-start | bytes 196
  428.0 20.5 %copy-start.8 = (s32[16]{0:T(128)S(1)}, s32[16]{0:T(128)}, u32[]{:S(2)}) copy-start(s32[16]{0:T(128)} %param.10) | copy-start | bytes 196
  428.0 21.5 %copy-start.1 = (f32[96,128]{1,0:T(8,128)S(1)}, f32[96,128]{1,0:T(8,128)}, u32[]{:S(2)}) copy-start(f32[96,128]{1,0:T(8,128)} %param.12) | copy-start | bytes 147460
